TPU v7x, 512 devices: a whole 4x8x8 slice. The times are simulated.
512 devices in a mesh: dp: 8 (over y_hi, x), expert: 64 (over y_lo, z, core).
Axes of the slice: x: 4, y: 8 (y_hi: 2, y_lo: 4; y = y_hi * 4 + y_lo), z: 8, core: 2. Of those that a mesh axis runs over, the one named last changes fastest.
Arguments:
- tokens: bfloat16 [8192, 2560], P(('dp', 'expert')), may hold values from -6 to 6
- grad_out: bfloat16 [8192, 2560], P(('dp', 'expert')), may hold values from -6 to 6
- expert_ids: int32 [8192, 2], P(('dp', 'expert')), may hold values from 0 to 63, as said below
- gates: bfloat16 [8192, 2], P(('dp', 'expert')), may hold values from 0.099609375 to 1
- w_gate: bfloat16 [64, 2560, 1024], P('expert', None, 'dp'), may hold values from -0.125 to 0.125
- w_up: bfloat16 [64, 2560, 1024], P('expert', None, 'dp'), may hold values from -0.125 to 0.125
- w_down: bfloat16 [64, 1024, 2560], P('expert', 'dp'), may hold values from -0.1875 to 0.1875
Outputs:
- out_tokens: bfloat16 [8192, 2560], P(('dp', 'expert'))
- grad_tokens: bfloat16 [8192, 2560], P(('dp', 'expert'))
- grad_gate: bfloat16 [64, 2560, 1024], P('expert', None, 'dp')
- grad_up: bfloat16 [64, 2560, 1024], P('expert', None, 'dp')
- grad_down: bfloat16 [64, 1024, 2560], P('expert', 'dp')
Inputs may be any that keep to these rules, and one draw needn't show every extreme that they name: `expert_ids`: each token names 2 different experts. Over the tokens of all devices at one index of expert taken together, one expert, the same at every index, is named exactly 8 times; a second one, also the same at every index, exactly 5 times; every other expert at most 5 times.
All inputs are finite; a program needn't handle non-finite values.
Results may differ from a plain program's by a relative error of at most 0.019.
Values may be sent and summed in bfloat16 or wider, within the bound.
No kernel may reach another device: no remote copies, remote signals or barrier semaphores. Data moves between devices by JAX's collectives and lax.ppermute only.
A program may use at most 128 MiB of HBM per device.

v0:
```python
import jax
import jax.numpy as jnp
from jax import lax
from jax.sharding import PartitionSpec as P


def expert_rows(rows_in, cot_in, gate_weight, up_weight, down_weight):
    gate_pre = jnp.dot(rows_in, gate_weight, preferred_element_type=jnp.float32)
    up_pre = jnp.dot(rows_in, up_weight, preferred_element_type=jnp.float32)
    hidden = (jax.nn.silu(gate_pre) * up_pre).astype(jnp.bfloat16)
    partial_value = jnp.dot(hidden, down_weight, preferred_element_type=jnp.float32).astype(
        jnp.bfloat16
    )
    first_dim = (((0,), (0,)), ((), ()))
    last_dim = (((1,), (1,)), ((), ()))
    grad_down = lax.dot_general(hidden, cot_in, first_dim, preferred_element_type=jnp.float32)
    d_hidden = lax.dot_general(cot_in, down_weight, last_dim, preferred_element_type=jnp.float32)
    sig = jax.nn.sigmoid(gate_pre)
    d_gate = (d_hidden * up_pre * sig * (1.0 + gate_pre * (1.0 - sig))).astype(jnp.bfloat16)
    d_up = (d_hidden * gate_pre * sig).astype(jnp.bfloat16)
    grad_gate = lax.dot_general(rows_in, d_gate, first_dim, preferred_element_type=jnp.float32)
    grad_up = lax.dot_general(rows_in, d_up, first_dim, preferred_element_type=jnp.float32)
    back_term = lax.dot_general(d_gate, gate_weight, last_dim, preferred_element_type=jnp.float32)
    back_term = (
        back_term + lax.dot_general(d_up, up_weight, last_dim, preferred_element_type=jnp.float32)
    ).astype(jnp.bfloat16)
    return (partial_value, back_term, grad_gate, grad_up, grad_down)


def fill_slots(slot_index, slot_total, assigned, top_count, group_tokens, cot_rows):
    owner = jnp.full((slot_total,), assigned, jnp.int32)
    owner = owner.at[slot_index].set(jnp.arange(assigned, dtype=jnp.int32), mode="drop")
    filled = owner < assigned
    safe = jnp.where(filled, owner, 0)
    token_rows = jnp.take(group_tokens, safe // top_count, axis=0)
    cot_taken = jnp.take(cot_rows, safe, axis=0)
    token_rows = jnp.where(filled[:, None], token_rows, jnp.zeros((), token_rows.dtype))
    cot_taken = jnp.where(filled[:, None], cot_taken, jnp.zeros((), cot_taken.dtype))
    return (token_rows, cot_taken)


def collect_slots(values, slot_index, weights):
    taken = jnp.take(values, slot_index.reshape(-1), axis=0, mode="fill", fill_value=0)
    taken = taken.reshape(slot_index.shape[0], slot_index.shape[1], values.shape[1]).astype(
        jnp.float32
    )
    if weights is None:
        return jnp.sum(taken, axis=1)
    return jnp.sum(weights.astype(jnp.float32)[:, :, None] * taken, axis=1)


def body(tokens, grad_out, expert_ids, gates, w_gate, w_up, w_down):
    dp_count = lax.axis_size("dp")
    experts = lax.axis_size("expert")
    local_rows = tokens.shape[0]
    feature_width = tokens.shape[1]
    top_count = expert_ids.shape[1]
    group_rows = dp_count * local_rows
    assigned = group_rows * top_count
    mean_slots = assigned // experts
    cap_hot = 2 * mean_slots
    group_tokens, group_grads, group_ids, group_gates = (
        lax.all_gather(tokens, "dp", axis=0, tiled=True),
        lax.all_gather(grad_out, "dp", axis=0, tiled=True),
        lax.all_gather(expert_ids, "dp", axis=0, tiled=True),
        lax.all_gather(gates, "dp", axis=0, tiled=True),
    )
    flat_ids = group_ids.reshape(-1)
    expert_range = jnp.arange(experts, dtype=jnp.int32)
    member = (flat_ids[:, None] == expert_range[None, :]).astype(jnp.int32)
    before = jnp.sum((jnp.cumsum(member, axis=0) - member) * member, axis=1)
    cot_rows = (
        (group_gates.astype(jnp.float32)[:, :, None] * group_grads.astype(jnp.float32)[:, None, :])
        .astype(jnp.bfloat16)
        .reshape(assigned, feature_width)
    )
    goes_out = jnp.ones(flat_ids.shape, dtype=bool)
    slot_count = experts * cap_hot
    slot_of = jnp.where(goes_out, flat_ids * cap_hot + before, slot_count).astype(jnp.int32)
    send_rows, send_cot = fill_slots(
        slot_of, slot_count, assigned, top_count, group_tokens, cot_rows
    )
    arrived_rows, arrived_cot = (
        lax.all_to_all(
            send_rows.reshape(experts, cap_hot, feature_width),
            "expert",
            split_axis=0,
            concat_axis=0,
            tiled=True,
        ),
        lax.all_to_all(
            send_cot.reshape(experts, cap_hot, feature_width),
            "expert",
            split_axis=0,
            concat_axis=0,
            tiled=True,
        ),
    )
    partial_value, back_term, grad_gate, grad_up, grad_down = expert_rows(
        arrived_rows.reshape(slot_count, feature_width),
        arrived_cot.reshape(slot_count, feature_width),
        w_gate[0],
        w_up[0],
        w_down[0],
    )
    return_partial, return_back = (
        lax.all_to_all(
            partial_value.reshape(experts, cap_hot, feature_width),
            "expert",
            split_axis=0,
            concat_axis=0,
            tiled=True,
        ),
        lax.all_to_all(
            back_term.reshape(experts, cap_hot, feature_width),
            "expert",
            split_axis=0,
            concat_axis=0,
            tiled=True,
        ),
    )
    slot_pairs = slot_of.reshape(group_rows, top_count)
    out_part = collect_slots(
        return_partial.reshape(slot_count, feature_width), slot_pairs, group_gates
    )
    back_part = collect_slots(return_back.reshape(slot_count, feature_width), slot_pairs, None)
    out_sum, back_sum = (
        lax.psum_scatter(
            out_part.astype(jnp.bfloat16), "dp", scatter_dimension=0, tiled=True
        ).astype(jnp.float32),
        lax.psum_scatter(
            back_part.astype(jnp.bfloat16), "dp", scatter_dimension=0, tiled=True
        ).astype(jnp.float32),
    )
    return (
        out_sum.astype(jnp.bfloat16),
        back_sum.astype(jnp.bfloat16),
        grad_gate.astype(jnp.bfloat16)[None],
        grad_up.astype(jnp.bfloat16)[None],
        grad_down.astype(jnp.bfloat16)[None],
    )


def solution(mesh):
    in_specs = (
        P(("dp", "expert"), None),
        P(("dp", "expert"), None),
        P(("dp", "expert"), None),
        P(("dp", "expert"), None),
        P("expert", None, "dp"),
        P("expert", None, "dp"),
        P("expert", "dp", None),
    )
    out_specs = (
        P(("dp", "expert"), None),
        P(("dp", "expert"), None),
        P("expert", None, "dp"),
        P("expert", None, "dp"),
        P("expert", "dp", None),
    )
    return jax.shard_map(body, mesh=mesh, in_specs=in_specs, out_specs=out_specs, check_vma=False)
```

profile of v0, /device:TPU:2, one launch (start us, length us, event | category | flops | bytes accessed | tf_op | source)
XLA Modules:
  0.0 699.0 jit_solution(2245142333885996936)
XLA Ops:
  7.2 29.1 %all-gather.1 = s32[8,16,2]{1,2,0:T(2,128)S(1)} all-gather(s32[1,16,2]{1,2,0:T(2,128)} %bitcast.86), channel_id=1, replica_groups=mesh['dp'=8,'expert'=64] {'dp'}, dimensions={0}, use_global_device_ids=true | all-gather | bytes 1152 | tf_op jit(solution)/shard_map/all_gather | solution.py:65
  36.3 0.1 copy.28
  36.5 0.1 eq.25
  36.6 0.1 eq.29
  36.7 0.1 copy.32
  36.9 0.1 mul.77
  37.0 0.6 reduce-window.6
  37.6 0.2 slice_reduce_fusion
  38.0 1.4 scatter_custom_fusion
  39.4 25.7 %all-gather = bf16[8,16,2]{1,2,0:T(2,128)(2,1)S(1)} all-gather(bf16[1,16,2]{1,2,0:T(2,128)(2,1)} %bitcast.88), channel_id=1, replica_groups=mesh['dp'=8,'expert'=64] {'dp'}, dimensions={0}, use_global_device_ids=true | all-gather | bytes 576 | tf_op jit(solution)/shard_map/all_gather | solution.py:66
  65.2 0.1 copy.34
  65.3 0.1 mul.84
  65.7 0.3 copy-done.3
  66.0 40.3 %all_gather.14 = bf16[128,2560]{1,0:T(8,128)(2,1)S(1)} all-gather(bf16[16,2560]{1,0:T(8,128)(2,1)} %param.9), channel_id=1, replica_groups=mesh['dp'=8,'expert'=64] {'dp'}, dimensions={0}, use_global_device_ids=true | all-gather | bytes 737280 | tf_op jit(solution)/shard_map/all_gather | solution.py:63
  106.4 46.3 %all_gather.15 = bf16[128,2560]{1,0:T(8,128)(2,1)S(1)} all-gather(bf16[16,2560]{1,0:T(8,128)(2,1)} %param.10), channel_id=1, replica_groups=mesh['dp'=8,'expert'=64] {'dp'}, dimensions={0}, use_global_device_ids=true | all-gather | bytes 737280 | tf_op jit(solution)/shard_map/all_gather | solution.py:64
  152.7 2.2 mul.86
  154.9 4.5 mul.87
  159.4 3.5 gather_fusion
  162.9 1.9 multiply_convert_fusion
  164.9 3.5 gather_fusion.1
  168.4 4.0 fusion.8
  172.3 73.2 %all_to_all.20 = bf16[64,8,2560]{2,1,0:T(8,128)(2,1)S(1)} all-to-all(bf16[64,8,2560]{2,1,0:T(8,128)(2,1)S(1)} %get-tuple-element.14), channel_id=1, replica_groups=mesh['dp'=8,'expert'=64] {'expert'}, dimensions={0} | all-to-all | bytes 5242880 | tf_op jit(solution)/shard_map/all_to_all | solution.py:84
  245.5 12.7 %all-to-all-start.2 = ((bf16[64,8,2560]{2,1,0:T(8,128)(2,1)}), bf16[64,8,2560]{2,1,0:T(8,128)(2,1)}, u32[]{:S(2)}, u32[]{:S(2)}) async-start(bf16[64,8,2560]{2,1,0:T(8,128)(2,1)} %get-tuple-element.13), calls=%async_computation.3 | async-start | bytes 5242880 | tf_op jit(solution)/shard_map/all_to_all | solution.py:91
  258.2 2.0 fusion.11
  260.2 1.5 fusion.13
  261.8 58.2 %all-to-all-done.2 = bf16[64,8,2560]{2,1,0:T(8,128)(2,1)} async-done(((bf16[64,8,2560]{2,1,0:T(8,128)(2,1)}), bf16[64,8,2560]{2,1,0:T(8,128)(2,1)}, u32[]{:S(2)}, u32[]{:S(2)}) %all-to-all-start.2) | async-done | bytes 2621472 | tf_op jit(solution)/shard_map/all_to_all | solution.py:91
  319.9 3.3 multiply_convert_fusion.1
  323.2 0.6 copy-done.7
  323.9 2.3 fusion.1
  326.2 16.2 %all-to-all-start.1 = ((bf16[64,8,2560]{2,1,0:T(8,128)(2,1)}), bf16[64,8,2560]{2,1,0:T(8,128)(2,1)}, u32[]{:S(2)}, u32[]{:S(2)}) async-start(bf16[64,8,2560]{2,1,0:T(8,128)(2,1)} %fusion.1), calls=%async_computation.1 | async-start | bytes 5242880 | tf_op jit(solution)/shard_map/all_to_all | solution.py:107
  342.4 2.1 fusion.20
  344.5 2.4 fusion
  347.0 57.2 %all-to-all-done.1 = bf16[64,8,2560]{2,1,0:T(8,128)(2,1)} async-done(((bf16[64,8,2560]{2,1,0:T(8,128)(2,1)}), bf16[64,8,2560]{2,1,0:T(8,128)(2,1)}, u32[]{:S(2)}, u32[]{:S(2)}) %all-to-all-start.1) | async-done | bytes 2621472 | tf_op jit(solution)/shard_map/all_to_all | solution.py:107
  404.2 16.2 %all-to-all-start.3 = ((bf16[64,8,2560]{2,1,0:T(8,128)(2,1)}), bf16[64,8,2560]{2,1,0:T(8,128)(2,1)}, u32[]{:S(2)}, u32[]{:S(2)}) async-start(bf16[64,8,2560]{2,1,0:T(8,128)(2,1)} %fusion), calls=%async_computation.4 | async-start | bytes 5242880 | tf_op jit(solution)/shard_map/all_to_all | solution.py:114
  420.4 5.9 gather_fusion.2
  426.3 55.8 %all-to-all-done.3 = bf16[64,8,2560]{2,1,0:T(8,128)(2,1)} async-done(((bf16[64,8,2560]{2,1,0:T(8,128)(2,1)}), bf16[64,8,2560]{2,1,0:T(8,128)(2,1)}, u32[]{:S(2)}, u32[]{:S(2)}) %all-to-all-start.3) | async-done | bytes 2621472 | tf_op jit(solution)/shard_map/all_to_all | solution.py:114
  482.1 6.0 gather_fusion.3
  488.1 4.0 broadcast_select_fusion
  492.1 4.0 reshape.131
  496.1 5.4 reduce_sum.35
  501.5 0.3 reduce-scatter.3.cloned.1.call-start
  501.8 4.4 reshape.132
  506.2 6.3 multiply_reduce_fusion
  512.5 3.2 fusion.4
  515.7 1.7 fusion.3
  517.4 1.7 fusion.2
  519.2 80.9 %reduce-scatter.5.cloned.1.call-done = bf16[16,2560]{1,0:T(8,128)(2,1)} async-done(((bf16[128,2560]{1,0:T(8,128)(2,1)}), bf16[16,2560]{1,0:T(8,128)(2,1)}) %reduce-scatter.5.cloned.1.call-update) | async-done | bytes 81936 | tf_op jit(solution)/shard_map/reduce_scatter | solution.py:131
  600.1 92.1 %reduce-scatter.3.cloned.1.call-done = bf16[16,2560]{1,0:T(8,128)(2,1)} async-done(((bf16[128,2560]{1,0:T(8,128)(2,1)}), bf16[16,2560]{1,0:T(8,128)(2,1)}) %reduce-scatter.3.cloned.1.call-update) | async-done | bytes 81936 | tf_op jit(solution)/shard_map/reduce_scatter | solution.py:128
  (34 shorter events, 0.6 us)
Async XLA Ops:
  7.2 312.8 %copy-start = (bf16[1,128,2560]{2,1,0:T(8,128)(2,1)S(1)}, bf16[1,128,2560]{2,1,0:T(8,128)(2,1)}, u32[]{:S(2)}) copy-start(bf16[1,128,2560]{2,1,0:T(8,128)(2,1)} %param.15) | copy-start | bytes 1966084
  65.3 0.6 copy-start.3
  245.5 74.4 %all-to-all-start.2 = ((bf16[64,8,2560]{2,1,0:T(8,128)(2,1)}), bf16[64,8,2560]{2,1,0:T(8,128)(2,1)}, u32[]{:S(2)}, u32[]{:S(2)}) async-start(bf16[64,8,2560]{2,1,0:T(8,128)(2,1)} %get-tuple-element.13), calls=%async_computation.3 | async-start | bytes 5242880 | tf_op jit(solution)/shard_map/all_to_all | solution.py:91
  258.2 2.0 copy-start.2
  323.2 0.6 copy-start.7
  326.2 77.9 %all-to-all-start.1 = ((bf16[64,8,2560]{2,1,0:T(8,128)(2,1)}), bf16[64,8,2560]{2,1,0:T(8,128)(2,1)}, u32[]{:S(2)}, u32[]{:S(2)}) async-start(bf16[64,8,2560]{2,1,0:T(8,128)(2,1)} %fusion.1), calls=%async_computation.1 | async-start | bytes 5242880 | tf_op jit(solution)/shard_map/all_to_all | solution.py:107
  342.4 2.1 copy-start.1
  342.4 2.1 copy-start.5
  404.2 77.9 %all-to-all-start.3 = ((bf16[64,8,2560]{2,1,0:T(8,128)(2,1)}), bf16[64,8,2560]{2,1,0:T(8,128)(2,1)}, u32[]{:S(2)}, u32[]{:S(2)}) async-start(bf16[64,8,2560]{2,1,0:T(8,128)(2,1)} %fusion), calls=%async_computation.4 | async-start | bytes 5242880 | tf_op jit(solution)/shard_map/all_to_all | solution.py:114
  420.4 179.7 %reduce-scatter.5.cloned.1.call-start = ((), (), s32[]{:S(2)}) async-start(), calls=%async_computation.7 | async-start | bytes 737280 | tf_op jit(solution)/shard_map/reduce_scatter | solution.py:131
  501.5 190.7 %reduce-scatter.3.cloned.1.call-start = ((), (), s32[]{:S(2)}) async-start(), calls=%async_computation.6 | async-start | bytes 737280 | tf_op jit(solution)/shard_map/reduce_scatter | solution.py:128
  501.7 4.4 copy-start.4
  515.7 1.7 copy-start.6
Sparse Core Ops, SparseCore 0:
  501.6 98.4 reduce-scatter.4
  605.1 86.9 reduce-scatter.2
where the time goes:
time: 700 us; the launch traced here: 699 us
  waiting for transfers between devices  344 us (49%)
  blocking collectives  215 us (31%)
  starting transfers between devices  45.4 us (6%)
  local copies, waits for them, and re-layouts  37.7 us (5%)
  other arithmetic  22.5 us (3%)
  matrix products  20.3 us (3%)
  between operations  14.3 us (2%)
    reduce_scatter x1, waiting for transfers between devices, body(): lax.psum_scatter(out_part.astype(jnp.bfloat16), 'dp', scatter_dimension=0...  92.1 us
    reduce_scatter x1, waiting for transfers between devices, body(): lax.psum_scatter(back_part.astype(jnp.bfloat16), 'dp', scatter_dimension=...  80.9 us
    all_to_all x1, blocking collectives, body(): lax.all_to_all(send_rows.reshape(experts, cap_hot, feature_width), 'exper...  73.2 us
    all_to_all x1, waiting for transfers between devices, body(): lax.all_to_all(send_cot.reshape(experts, cap_hot, feature_width), 'expert...  58.2 us
    all_to_all x1, waiting for transfers between devices, body(): lax.all_to_all(partial_value.reshape(experts, cap_hot, feature_width), 'e...  57.2 us
    all_to_all x1, waiting for transfers between devices, body(): lax.all_to_all(back_term.reshape(experts, cap_hot, feature_width), 'exper...  55.8 us
    all_gather x1, blocking collectives, body(): lax.all_gather(grad_out, 'dp', axis=0, tiled=True)  46.3 us
    all_gather x1, blocking collectives, body(): lax.all_gather(tokens, 'dp', axis=0, tiled=True)  40.3 us
  transfers between devices with their start and end apart: 5, of which 5 were waited for; matrix products, arithmetic and copies ran while one was open for 4% of the time, Pallas kernels for 0%

commit v1 on v0

--- a/solution.py
+++ b/solution.py
@@ -2,6 +2,13 @@
 import jax.numpy as jnp
 from jax import lax
 from jax.sharding import PartitionSpec as P
+
+end_series_now = lambda my_data, k_dim: jnp.concatenate(
+    lax.all_to_all(
+        jnp.stack(lax.axis_size("dp") * [my_data]), axis_name="dp", split_axis=0, concat_axis=0
+    ),
+    axis=k_dim,
+)
 
 
 def expert_rows(rows_in, cot_in, gate_weight, up_weight, down_weight):
@@ -61,7 +68,7 @@
     cap_hot = 2 * mean_slots
     group_tokens, group_grads, group_ids, group_gates = (
         lax.all_gather(tokens, "dp", axis=0, tiled=True),
-        lax.all_gather(grad_out, "dp", axis=0, tiled=True),
+        end_series_now(grad_out, 0),
         lax.all_gather(expert_ids, "dp", axis=0, tiled=True),
         lax.all_gather(gates, "dp", axis=0, tiled=True),
     )

time: 700 us -> 671 us (0.959)
  blocking collectives: 215 us -> 172 us
  starting transfers between devices: 45.4 us -> 56.3 us
  waiting for transfers between devices: 344 us -> 351 us
    all_gather x1 -> x0, blocking collectives: 46.3 us -> none  [body(): lax.all_gather(grad_out, 'dp', axis=0, tiled=True)]
    reduce_scatter x1, waiting for transfers between devices: 80.9 us -> 92.1 us  [body(): lax.psum_scatter(back_part.astype(jnp.bfloat16), 'dp', scatter_dimension=...]
    all_to_all x0 -> x1, starting transfers between devices: none -> 10.1 us  [lax.all_to_all(jnp.stack(lax.axis_size('dp') * [my_data]), axis_name='dp'...]
  transfers between devices with their start and end apart: 5 -> 6, of which waited for: 5 -> 5; matrix products, arithmetic and copies ran while one was open for 4% -> 5% of each run, Pallas kernels for 0% -> 0%
where the time goes in v1:
time: 671 us; the launch traced here: 670 us
  waiting for transfers between devices  351 us (52%)
  blocking collectives  172 us (26%)
  starting transfers between devices  56.3 us (8%)
  local copies, waits for them, and re-layouts  36.4 us (5%)
  other arithmetic  22.5 us (3%)
  matrix products  19 us (3%)
  between operations  14.3 us (2%)
    reduce_scatter x1, waiting for transfers between devices, body(): lax.psum_scatter(back_part.astype(jnp.bfloat16), 'dp', scatter_dimension=...  92.1 us
    reduce_scatter x1, waiting for transfers between devices, body(): lax.psum_scatter(out_part.astype(jnp.bfloat16), 'dp', scatter_dimension=0...  85.3 us
    all_to_all x1, blocking collectives, body(): lax.all_to_all(send_rows.reshape(experts, cap_hot, feature_width), 'exper...  75.1 us
    all_to_all x1, waiting for transfers between devices, body(): lax.all_to_all(back_term.reshape(experts, cap_hot, feature_width), 'exper...  59.4 us
    all_to_all x1, waiting for transfers between devices, body(): lax.all_to_all(send_cot.reshape(experts, cap_hot, feature_width), 'expert...  58.2 us
    all_to_all x1, waiting for transfers between devices, body(): lax.all_to_all(partial_value.reshape(experts, cap_hot, feature_width), 'e...  55.6 us
    all_gather x1, blocking collectives, body(): lax.all_gather(tokens, 'dp', axis=0, tiled=True)  40.1 us
    all_gather x1, blocking collectives, body(): lax.all_gather(expert_ids, 'dp', axis=0, tiled=True)  33.6 us
  transfers between devices with their start and end apart: 6, of which 5 were waited for; matrix products, arithmetic and copies ran while one was open for 5% of the time, Pallas kernels for 0%

profile of v1, /device:TPU:2, one launch (start us, length us, event | category | flops | bytes accessed | tf_op | source)
XLA Modules:
  0.0 670.4 jit_solution(1115932848486051379)
XLA Ops:
  7.2 1.8 stack.2
  9.0 10.1 %all-to-all-start.2 = ((bf16[8,16,2560]{2,1,0:T(8,128)(2,1)}), bf16[8,16,2560]{2,1,0:T(8,128)(2,1)S(1)}, u32[]{:S(2)}, u32[]{:S(2)}) async-start(bf16[8,16,2560]{2,1,0:T(8,128)(2,1)} %stack.2), calls=%async_computation.3 | async-start | bytes 1310720 | tf_op jit(solution)/shard_map/all_to_all | solution.py:7
  19.1 33.6 %all-gather.1 = s32[8,16,2]{1,2,0:T(2,128)S(1)} all-gather(s32[1,16,2]{1,2,0:T(2,128)} %bitcast.88), channel_id=1, replica_groups=mesh['dp'=8,'expert'=64] {'dp'}, dimensions={0}, use_global_device_ids=true | all-gather | bytes 1152 | tf_op jit(solution)/shard_map/all_gather | solution.py:72
  52.9 0.1 eq.29
  53.0 0.1 eq.25
  53.2 0.6 reduce-window.6
  53.8 0.2 slice_reduce_fusion
  54.2 0.1 mul.77
  54.4 1.4 scatter_custom_fusion
  56.2 22.7 %all-gather = bf16[8,16,2]{1,2,0:T(2,128)(2,1)S(1)} all-gather(bf16[1,16,2]{1,2,0:T(2,128)(2,1)S(1)} %bitcast.90), channel_id=1, replica_groups=mesh['dp'=8,'expert'=64] {'dp'}, dimensions={0}, use_global_device_ids=true | all-gather | bytes 576 | tf_op jit(solution)/shard_map/all_gather | solution.py:73
  79.0 0.1 mul.84
  79.1 0.5 copy-done.4
  79.6 40.1 %all_gather.11 = bf16[128,2560]{1,0:T(8,128)(2,1)S(1)} all-gather(bf16[16,2560]{1,0:T(8,128)(2,1)S(1)} %copy-done.11), channel_id=1, replica_groups=mesh['dp'=8,'expert'=64] {'dp'}, dimensions={0}, use_global_device_ids=true | all-gather | bytes 737280 | tf_op jit(solution)/shard_map/all_gather | solution.py:70
  119.7 3.5 gather_fusion
  123.2 0.2 bitcast_convert_fusion
  123.4 0.9 mul.86
  124.3 2.9 mul.87
  127.2 1.9 multiply_convert_fusion
  129.1 3.5 gather_fusion.1
  132.6 3.9 fusion.8
  136.5 75.1 %all_to_all.25 = bf16[64,8,2560]{2,1,0:T(8,128)(2,1)S(1)} all-to-all(bf16[64,8,2560]{2,1,0:T(8,128)(2,1)S(1)} %get-tuple-element.14), channel_id=1, replica_groups=mesh['dp'=8,'expert'=64] {'expert'}, dimensions={0} | all-to-all | bytes 5242880 | tf_op jit(solution)/shard_map/all_to_all | solution.py:91
  211.7 12.9 %all-to-all-start.3 = ((bf16[64,8,2560]{2,1,0:T(8,128)(2,1)}), bf16[64,8,2560]{2,1,0:T(8,128)(2,1)}, u32[]{:S(2)}, u32[]{:S(2)}) async-start(bf16[64,8,2560]{2,1,0:T(8,128)(2,1)} %get-tuple-element.13), calls=%async_computation.4 | async-start | bytes 5242880 | tf_op jit(solution)/shard_map/all_to_all | solution.py:98
  224.5 2.0 fusion.11
  226.5 1.5 fusion.13
  228.1 58.2 %all-to-all-done.3 = bf16[64,8,2560]{2,1,0:T(8,128)(2,1)} async-done(((bf16[64,8,2560]{2,1,0:T(8,128)(2,1)}), bf16[64,8,2560]{2,1,0:T(8,128)(2,1)}, u32[]{:S(2)}, u32[]{:S(2)}) %all-to-all-start.3) | async-done | bytes 2621472 | tf_op jit(solution)/shard_map/all_to_all | solution.py:98
  286.3 3.3 multiply_convert_fusion.1
  289.6 0.8 fusion.20
  290.5 0.3 copy-done.1
  290.8 2.4 fusion
  293.1 16.5 %all-to-all-start.4 = ((bf16[64,8,2560]{2,1,0:T(8,128)(2,1)}), bf16[64,8,2560]{2,1,0:T(8,128)(2,1)}, u32[]{:S(2)}, u32[]{:S(2)}) async-start(bf16[64,8,2560]{2,1,0:T(8,128)(2,1)} %fusion), calls=%async_computation.5 | async-start | bytes 5242880 | tf_op jit(solution)/shard_map/all_to_all | solution.py:121
  309.7 2.4 fusion.1
  312.1 59.4 %all-to-all-done.4 = bf16[64,8,2560]{2,1,0:T(8,128)(2,1)} async-done(((bf16[64,8,2560]{2,1,0:T(8,128)(2,1)}), bf16[64,8,2560]{2,1,0:T(8,128)(2,1)}, u32[]{:S(2)}, u32[]{:S(2)}) %all-to-all-start.4) | async-done | bytes 2621472 | tf_op jit(solution)/shard_map/all_to_all | solution.py:121
  371.4 16.2 %all-to-all-start.1 = ((bf16[64,8,2560]{2,1,0:T(8,128)(2,1)}), bf16[64,8,2560]{2,1,0:T(8,128)(2,1)}, u32[]{:S(2)}, u32[]{:S(2)}) async-start(bf16[64,8,2560]{2,1,0:T(8,128)(2,1)} %fusion.1), calls=%async_computation.1 | async-start | bytes 5242880 | tf_op jit(solution)/shard_map/all_to_all | solution.py:114
  387.6 0.3 reduce-scatter.3.cloned.1.call-start
  387.9 5.9 gather_fusion.3
  393.8 55.6 %all-to-all-done.1 = bf16[64,8,2560]{2,1,0:T(8,128)(2,1)} async-done(((bf16[64,8,2560]{2,1,0:T(8,128)(2,1)}), bf16[64,8,2560]{2,1,0:T(8,128)(2,1)}, u32[]{:S(2)}, u32[]{:S(2)}) %all-to-all-start.1) | async-done | bytes 2621472 | tf_op jit(solution)/shard_map/all_to_all | solution.py:114
  449.3 5.9 gather_fusion.2
  455.3 3.9 broadcast_select_fusion
  459.2 4.4 reshape.141
  463.6 6.3 multiply_reduce_fusion
  470.0 0.3 reduce-scatter.5.cloned.1.call-start
  470.3 4.0 reshape.140
  474.2 5.3 reduce_sum.35
  479.6 3.1 fusion.4
  482.7 1.7 fusion.2
  484.5 1.7 fusion.3
  486.2 85.3 %reduce-scatter.3.cloned.1.call-done = bf16[16,2560]{1,0:T(8,128)(2,1)} async-done(((bf16[128,2560]{1,0:T(8,128)(2,1)}), bf16[16,2560]{1,0:T(8,128)(2,1)}) %reduce-scatter.3.cloned.1.call-update) | async-done | bytes 81936 | tf_op jit(solution)/shard_map/reduce_scatter | solution.py:135
  571.5 92.1 %reduce-scatter.5.cloned.1.call-done = bf16[16,2560]{1,0:T(8,128)(2,1)} async-done(((bf16[128,2560]{1,0:T(8,128)(2,1)}), bf16[16,2560]{1,0:T(8,128)(2,1)}) %reduce-scatter.5.cloned.1.call-update) | async-done | bytes 81936 | tf_op jit(solution)/shard_map/reduce_scatter | solution.py:138
  (47 shorter events, 1.0 us)
Async XLA Ops:
  7.2 279.1 %copy-start = (bf16[1,128,2560]{2,1,0:T(8,128)(2,1)S(1)}, bf16[1,128,2560]{2,1,0:T(8,128)(2,1)}, u32[]{:S(2)}) copy-start(bf16[1,128,2560]{2,1,0:T(8,128)(2,1)} %param.15) | copy-start | bytes 1966084
  7.2 49.0 %copy-start.12 = (bf16[16,2]{0,1:T(2,128)(2,1)S(1)}, bf16[16,2]{0,1:T(2,128)(2,1)}, u32[]{:S(2)}) copy-start(bf16[16,2]{0,1:T(2,128)(2,1)} %param.12) | copy-start | bytes 196
  7.2 72.4 %copy-start.11 = (bf16[16,2560]{1,0:T(8,128)(2,1)S(1)}, bf16[16,2560]{1,0:T(8,128)(2,1)}, u32[]{:S(2)}) copy-start(bf16[16,2560]{1,0:T(8,128)(2,1)} %param.9) | copy-start | bytes 245764
  9.0 114.2 %all-to-all-start.2 = ((bf16[8,16,2560]{2,1,0:T(8,128)(2,1)}), bf16[8,16,2560]{2,1,0:T(8,128)(2,1)S(1)}, u32[]{:S(2)}, u32[]{:S(2)}) async-start(bf16[8,16,2560]{2,1,0:T(8,128)(2,1)} %stack.2), calls=%async_computation.3 | async-start | bytes 1310720 | tf_op jit(solution)/shard_map/all_to_all | solution.py:7
  79.0 0.6 copy-start.4
  211.7 74.6 %all-to-all-start.3 = ((bf16[64,8,2560]{2,1,0:T(8,128)(2,1)}), bf16[64,8,2560]{2,1,0:T(8,128)(2,1)}, u32[]{:S(2)}, u32[]{:S(2)}) async-start(bf16[64,8,2560]{2,1,0:T(8,128)(2,1)} %get-tuple-element.13), calls=%async_computation.4 | async-start | bytes 5242880 | tf_op jit(solution)/shard_map/all_to_all | solution.py:98
  224.5 2.0 copy-start.2
  286.3 3.3 copy-start.3
  289.6 0.9 copy-start.8
  289.6 0.9 copy-start.6
  289.6 1.2 copy-start.1
  293.1 16.5 %copy-start.10 = (bf16[512,128]{1,0:T(8,128)(2,1)S(1)}, bf16[512,128]{1,0:T(8,128)(2,1)}, u32[]{:S(2)}) copy-start(bf16[512,128]{1,0:T(8,128)(2,1)} %get-tuple-element.12) | copy-start | bytes 393220
  293.1 78.3 %all-to-all-start.4 = ((bf16[64,8,2560]{2,1,0:T(8,128)(2,1)}), bf16[64,8,2560]{2,1,0:T(8,128)(2,1)}, u32[]{:S(2)}, u32[]{:S(2)}) async-start(bf16[64,8,2560]{2,1,0:T(8,128)(2,1)} %fusion), calls=%async_computation.5 | async-start | bytes 5242880 | tf_op jit(solution)/shard_map/all_to_all | solution.py:121
  371.4 77.9 %all-to-all-start.1 = ((bf16[64,8,2560]{2,1,0:T(8,128)(2,1)}), bf16[64,8,2560]{2,1,0:T(8,128)(2,1)}, u32[]{:S(2)}, u32[]{:S(2)}) async-start(bf16[64,8,2560]{2,1,0:T(8,128)(2,1)} %fusion.1), calls=%async_computation.1 | async-start | bytes 5242880 | tf_op jit(solution)/shard_map/all_to_all | solution.py:114
  387.6 183.8 %reduce-scatter.3.cloned.1.call-start = ((), (), s32[]{:S(2)}) async-start(), calls=%async_computation.7 | async-start | bytes 737280 | tf_op jit(solution)/shard_map/reduce_scatter | solution.py:135
  459.2 4.4 copy-start.5
  470.0 193.6 %reduce-scatter.5.cloned.1.call-start = ((), (), s32[]{:S(2)}) async-start(), calls=%async_computation.8 | async-start | bytes 737280 | tf_op jit(solution)/shard_map/reduce_scatter | solution.py:138
  474.2 8.5 %copy-start.9 = (bf16[512,128]{1,0:T(8,128)(2,1)S(1)}, bf16[512,128]{1,0:T(8,128)(2,1)}, u32[]{:S(2)}) copy-start(bf16[512,128]{1,0:T(8,128)(2,1)} %copy-done.8) | copy-start | bytes 393220
  482.7 1.7 copy-start.7
Sparse Core Ops, SparseCore 0:
  470.1 101.3 reduce-scatter.2
  576.5 86.9 reduce-scatter.4
